TPU v7x, 32 devices: a whole 2x2x4 slice. The times are simulated.
32 devices in a mesh: dp: 8 (over z, y), seq: 4 (over x, core).
Axes of the slice: x: 2, y: 2, z: 4, core: 2. Of those that a mesh axis runs over, the one named last changes fastest.
Arguments:
- frames: bfloat16 [8, 512, 1536], P('dp', 'seq'), may hold values from -6 to 6
- lengths: int32 [8, 4], P('dp'), may hold values from 1 to 256, 512 in all within a row
- ln1_gain: float32 [1536], replicated, may hold values from 0.5 to 12
- ln2_gain: float32 [1536], replicated, may hold values from 0.5 to 1.5
- w_qkv: bfloat16 [1536, 3, 1536], P('dp', None, 'seq'), may hold values from -0.15625 to 0.15625
- w_out: bfloat16 [1536, 1536], P('seq', 'dp'), may hold values from -0.15625 to 0.15625
- w_glu: bfloat16 [1536, 2, 1536], P('dp', None, 'seq'), may hold values from -0.15625 to 0.15625
- dw_kernel: bfloat16 [31, 1536], P(None, 'seq'), may hold values from -1 to 1
- w_proj: bfloat16 [1536, 1536], P('seq', 'dp'), may hold values from -0.15625 to 0.15625
Outputs:
- block_out: bfloat16 [8, 512, 1536], P('dp', 'seq')
Inputs may be any that keep to these rules, and one draw needn't show every extreme that they name: `lengths`: each row sums to 512, and its largest entry is 256.
All inputs are finite; a program needn't handle non-finite values.
Results may differ from a plain program's by a relative error of at most 0.013.
The roundings to bfloat16 on the way count: a program that leaves them out, or rounds other values in their place, can miss the bound.
Values may be sent and summed in bfloat16 or wider, within the bound.
No kernel may reach another device: no remote copies, remote signals or barrier semaphores. Data moves between devices by JAX's collectives and lax.ppermute only.
A program may use at most 64 MiB of HBM per device.

v0:
```python
import jax
import jax.numpy as jnp
from jax import lax
from jax.sharding import PartitionSpec as P

HD = 96


def layer_norm(values, gain_vec):
    mean_value = jnp.mean(values, axis=-1, keepdims=True)
    centered = values - mean_value
    variance = jnp.mean(centered * centered, axis=-1, keepdims=True)
    return (centered * lax.rsqrt(variance + 1e-05) * gain_vec).astype(jnp.bfloat16)


def segment_of(record_ends, positions):
    return jnp.sum((positions[:, None] >= record_ends[None, :]).astype(jnp.int32), axis=1)


def attend(projected, seg_all, head_size):
    group_rows = projected.shape[0]
    block_rows = 512
    heads_here = projected.shape[2] // head_size
    split = projected.reshape(group_rows, 3, heads_here, head_size)
    queries = split[:, 0]
    keys = split[:, 1]
    values = split[:, 2]
    blocks = group_rows // block_rows
    scale = 1.0 / head_size**0.5

    def one_block(block_data):
        query_block, seg_block = block_data
        scores = (
            jnp.einsum("qhe,khe->hqk", query_block, keys, preferred_element_type=jnp.float32)
            * scale
        )
        allowed = seg_block[:, None] == seg_all[None, :]
        scores = jnp.where(allowed[None], scores, -1e30)
        top_score = jnp.max(scores, axis=-1, keepdims=True)
        weights = jnp.exp(scores - top_score)
        probs = (weights / jnp.sum(weights, axis=-1, keepdims=True)).astype(jnp.bfloat16)
        mixed = jnp.einsum("hqk,khe->qhe", probs, values, preferred_element_type=jnp.float32)
        return mixed.astype(jnp.bfloat16).reshape(block_rows, heads_here * head_size)

    result = lax.map(
        one_block,
        (
            queries.reshape(blocks, block_rows, heads_here, head_size),
            seg_all.reshape(blocks, block_rows),
        ),
    )
    return result.reshape(group_rows, heads_here * head_size)


def depthwise(padded, kernel, seg_here, seg_near, count):
    total_acc = jnp.zeros((count, padded.shape[1]), jnp.float32)
    for tap_index in range(kernel.shape[0]):
        window = padded[tap_index : tap_index + count].astype(jnp.float32)
        same = (seg_near[tap_index : tap_index + count] == seg_here)[:, None]
        total_acc = total_acc + jnp.where(same, window * kernel[tap_index].astype(jnp.float32), 0.0)
    return jax.nn.silu(total_acc).astype(jnp.bfloat16)


def on_device(frames, lengths, ln1_gain, ln2_gain, w_qkv, w_out, w_glu, dw_kernel, w_proj):
    frame_rows = frames.shape[1]
    model_width = frames.shape[2]
    seq_count = lax.axis_size("seq")
    group_rows = frame_rows * seq_count
    group_width = model_width // seq_count
    kernel_reach = dw_kernel.shape[0] // 2
    qkv_local = lax.all_gather(w_qkv, "dp", axis=0, tiled=True)
    out_local = lax.all_gather(w_out, "dp", axis=1, tiled=True)
    glu_local = lax.all_gather(w_glu, "dp", axis=0, tiled=True)
    proj_local = lax.all_gather(w_proj, "dp", axis=1, tiled=True)
    qkv_matrix = qkv_local.reshape(model_width, 3 * group_width)
    glu_matrix = glu_local.reshape(model_width, 2 * group_width)
    inputs = frames[0].astype(jnp.float32)
    record_ends = jnp.cumsum(lengths[0])
    seg_all = segment_of(record_ends, jnp.arange(group_rows, dtype=jnp.int32))
    normed1 = layer_norm(inputs, ln1_gain)
    projected = (
        jnp.dot(
            lax.all_gather(normed1, "seq", axis=0, tiled=True),
            qkv_matrix,
            preferred_element_type=jnp.float32,
        )
        .astype(jnp.bfloat16)
        .reshape(group_rows, 3, group_width)
    )
    attended = attend(projected, seg_all, HD)
    rows_here = attended
    attn_sum = lax.psum_scatter(
        jnp.dot(rows_here, out_local, preferred_element_type=jnp.float32)
        .astype(jnp.bfloat16)
        .astype(jnp.float32)
        .astype(jnp.bfloat16),
        "seq",
        scatter_dimension=0,
        tiled=True,
    ).astype(jnp.float32)
    middle = (inputs + attn_sum).astype(jnp.bfloat16)
    normed2 = layer_norm(middle.astype(jnp.float32), ln2_gain)
    shard_piece = lax.all_gather(normed2, "seq", axis=0, tiled=True)
    paired = jnp.dot(shard_piece, glu_matrix, preferred_element_type=jnp.float32).reshape(
        shard_piece.shape[0], 2, group_width
    )
    gated = (paired[:, 0] * jax.nn.sigmoid(paired[:, 1])).astype(jnp.bfloat16)
    padded = jnp.pad(gated, ((kernel_reach, kernel_reach), (0, 0)))
    near_positions = jnp.arange(-kernel_reach, group_rows + kernel_reach, dtype=jnp.int32)
    activated = depthwise(
        padded, dw_kernel, seg_all, segment_of(record_ends, near_positions), group_rows
    )
    rows_here = activated
    conv_out = lax.psum_scatter(
        jnp.dot(rows_here, proj_local, preferred_element_type=jnp.float32)
        .astype(jnp.bfloat16)
        .astype(jnp.float32)
        .astype(jnp.bfloat16),
        "seq",
        scatter_dimension=0,
        tiled=True,
    ).astype(jnp.float32)
    results = [(middle.astype(jnp.float32) + conv_out).astype(jnp.bfloat16)]
    return jnp.stack(results, axis=0)


def solution(mesh):
    in_specs = (
        P("dp", "seq", None),
        P("dp", None),
        P(),
        P(),
        P("dp", None, "seq"),
        P("seq", "dp"),
        P("dp", None, "seq"),
        P(None, "seq"),
        P("seq", "dp"),
    )
    out_specs = P("dp", "seq", None)
    return jax.shard_map(
        on_device, mesh=mesh, in_specs=in_specs, out_specs=out_specs, check_vma=False
    )
```

profile of v0, /device:TPU:0, one launch (start us, length us, event | category | flops | bytes accessed | tf_op | source)
XLA Modules:
  0.0 334.3 jit_solution(194160202395441783)
XLA Ops:
  6.5 0.7 all-gather.9.cloned.1.call-update
  7.3 0.0 all-gather.7.cloned.1.call-start
  7.3 1.1 convert_reduce_fusion.1
  8.4 1.2 fusion.19
  9.7 2.0 fusion.21
  11.7 0.0 all-gather.7.cloned.1.call-update
  11.8 0.0 all-gather.11.cloned.1.call-start
  11.8 0.7 all-gather.11.cloned.1.call-update
  12.5 0.0 reduce-scatter.3.cloned.1.call-start
  12.6 0.2 reduce-window.8
  12.7 0.1 convert_reduce_fusion.3
  12.8 0.2 broadcast_compare_fusion
  13.0 64.4 %all-gather.9.cloned.1.call-done = bf16[1536,3,384]{2,0,1:T(8,128)(2,1)} async-done(((bf16[192,3,384]{2,0,1:T(8,128)(2,1)}), bf16[1536,3,384]{2,0,1:T(8,128)(2,1)}) %all-gather.9.cloned.1.call-update) | async-done | bytes 3538960 | tf_op jit(solution)/shard_map/all_gather | solution.py:71
  77.5 6.1 %copy.23 = bf16[1536,3,384]{0,2,1:T(8,128)(2,1)} copy(bf16[1536,3,384]{2,0,1:T(8,128)(2,1)} %all-gather.9.cloned.1.call-done) | data formatting | bytes 7077888 | tf_op jit(solution)/shard_map/all_gather | solution.py:71
  83.6 13.6 %all-gather.7.cloned.1.call-done = bf16[512,1536]{1,0:T(8,128)(2,1)} async-done(((bf16[128,1536]{1,0:T(8,128)(2,1)}), bf16[512,1536]{1,0:T(8,128)(2,1)}) %all-gather.7.cloned.1.call-update) | async-done | bytes 1572880 | tf_op jit(solution)/shard_map/all_gather | solution.py:83
  97.2 4.7 %convolution_convert_fusion = bf16[512,1152]{1,0:T(8,128)(2,1)S(1)} fusion(bf16[512,1536]{1,0:T(8,128)(2,1)} %all-gather.7.cloned.1.call-done, bf16[1536,1152]{0,1:T(8,128)(2,1)} %bitcast.70), kind=kOutput, calls=%fused_computation.5 | convolution fusion | flops 1812529152 | bytes 6291456 | tf_op jit(solution)/shard_map/dot_general | solution.py:82
  101.9 0.6 copy.24
  102.5 3.6 %fusion.40 = (f32[4,512]{1,0:T(4,128)S(1)}, f32[4,512,512]{1,2,0:T(8,128)}) fusion(pred[512,512]{0,1:T(8,128)(4,1)S(1)} %broadcast_compare_fusion, bf16[512,3,4,96]{0,3,2,1:T(8,128)(2,1)S(1)} %bitcast.71), kind=kOutput, calls=%fused_computation.130 | convolution fusion | flops 205521408 | bytes 5251072 | tf_op jit(solution)/shard_map/while/body/eval_jaxpr/sub | solution.py:40
  106.2 2.8 fusion.9
  108.9 31.5 %all-gather.11.cloned.1.call-done = bf16[384,1536]{0,1:T(8,128)(2,1)} async-done(((bf16[384,192]{0,1:T(8,128)(2,1)}), bf16[384,1536]{0,1:T(8,128)(2,1)}) %all-gather.11.cloned.1.call-update) | async-done | bytes 1179664 | tf_op jit(solution)/shard_map/all_gather | solution.py:72
  140.5 3.5 %convolution_convert_fusion.2 = bf16[512,1536]{1,0:T(8,128)(2,1)} fusion(bf16[512,384]{0,1:T(8,128)(2,1)S(1)} %bitcast.73, bf16[384,1536]{0,1:T(8,128)(2,1)} %all-gather.11.cloned.1.call-done), kind=kOutput, calls=%fused_computation.7 | convolution fusion | flops 604766208 | bytes 3145728 | tf_op jit(solution)/shard_map/dot_general | solution.py:93
  144.0 0.0 reduce-scatter.3.cloned.1.call-update
  144.0 0.0 all-gather.15.cloned.1.call-start
  144.0 0.5 all-gather.15.cloned.1.call-update
  144.6 0.0 all-gather.13.cloned.1.call-start
  144.6 26.5 %reduce-scatter.3.cloned.1.call-done = bf16[128,1536]{1,0:T(8,128)(2,1)} async-done(((bf16[512,1536]{1,0:T(8,128)(2,1)}), bf16[128,1536]{1,0:T(8,128)(2,1)}) %reduce-scatter.3.cloned.1.call-update) | async-done | bytes 393232 | tf_op jit(solution)/shard_map/reduce_scatter | solution.py:92
  171.1 1.2 convert_reduce_fusion
  172.3 0.3 fusion.16
  172.6 1.0 fusion.18
  173.6 0.0 all-gather.13.cloned.1.call-update
  173.6 0.0 all-gather.17.cloned.1.call-start
  173.7 0.7 all-gather.17.cloned.1.call-update
  174.4 0.0 reduce-scatter.5.cloned.1.call-start
  174.4 0.1 convert_reduce_fusion.2
  174.5 0.1 convert_reduce_fusion.33
  174.6 0.1 convert_reduce_fusion.34
  174.7 0.1 slice_compare_fusion.29
  174.8 0.1 slice_compare_fusion.30
  174.9 50.6 %all-gather.15.cloned.1.call-done = bf16[1536,2,384]{2,1,0:T(2,128)(2,1)} async-done(((bf16[192,2,384]{2,1,0:T(2,128)(2,1)}), bf16[1536,2,384]{2,1,0:T(2,128)(2,1)}) %all-gather.15.cloned.1.call-update) | async-done | bytes 2359312 | tf_op jit(solution)/shard_map/all_gather | solution.py:73
  225.5 5.6 %copy.28 = bf16[1536,2,384]{0,2,1:T(8,128)(2,1)S(1)} copy(bf16[1536,2,384]{2,1,0:T(2,128)(2,1)} %all-gather.15.cloned.1.call-done) | data formatting | bytes 4718592 | tf_op jit(solution)/shard_map/reshape | solution.py:76
  231.1 14.1 %all-gather.13.cloned.1.call-done = bf16[512,1536]{1,0:T(8,128)(2,1)} async-done(((bf16[128,1536]{1,0:T(8,128)(2,1)}), bf16[512,1536]{1,0:T(8,128)(2,1)}) %all-gather.13.cloned.1.call-update) | async-done | bytes 1572880 | tf_op jit(solution)/shard_map/all_gather | solution.py:103
  245.2 2.8 fusion.2
  248.0 0.2 fusion.32
  248.2 40.5 %all-gather.17.cloned.1.call-done = bf16[384,1536]{0,1:T(8,128)(2,1)} async-done(((bf16[384,192]{0,1:T(8,128)(2,1)}), bf16[384,1536]{0,1:T(8,128)(2,1)}) %all-gather.17.cloned.1.call-update) | async-done | bytes 1179664 | tf_op jit(solution)/shard_map/all_gather | solution.py:74
  288.7 9.8 %convolution_convert_fusion.1 = bf16[512,1536]{1,0:T(8,128)(2,1)} fusion(bf16[384,1536]{0,1:T(8,128)(2,1)} %all-gather.17.cloned.1.call-done, bf16[512,384]{1,0:T(8,128)(2,1)S(1)} %fusion.32, f32[384]{0:T(512)S(1)} %get-tuple-element.55, f32[384]{0:T(512)S(1)} %get-tuple-element.56, f32[384]{0:T(512)S(1)} %get-tuple-element.18, ...), kind=kOutput, calls=%fused_computation.6 | convolution fusion | flops 629932032 | bytes 3209216 | tf_op jit(solution)/shard_map/dot_general | solution.py:115
  298.5 0.0 reduce-scatter.5.cloned.1.call-update
  298.5 27.1 %reduce-scatter.5.cloned.1.call-done = bf16[128,1536]{1,0:T(8,128)(2,1)} async-done(((bf16[512,1536]{1,0:T(8,128)(2,1)}), bf16[128,1536]{1,0:T(8,128)(2,1)}) %reduce-scatter.5.cloned.1.call-update) | async-done | bytes 393232 | tf_op jit(solution)/shard_map/reduce_scatter | solution.py:114
  325.6 1.8 fusion.31
  (14 shorter events, 0.1 us)
Async XLA Ops:
  6.5 6.0 %copy-start.3 = (s32[1,4]{1,0:T(1,128)S(1)}, s32[1,4]{1,0:T(1,128)}, u32[]{:S(2)}) copy-start(s32[1,4]{1,0:T(1,128)} %param.10) | copy-start | bytes 52
  6.5 70.9 %all-gather.9.cloned.1.call-start = ((), (), s32[]{:S(2)}) async-start(), calls=%async_computation.3 | async-start | bytes 3981312 | tf_op jit(solution)/shard_map/all_gather | solution.py:71
  7.3 89.9 %all-gather.7.cloned.1.call-start = ((), (), s32[]{:S(2)}) async-start(), calls=%async_computation.2 | async-start | bytes 1966080 | tf_op jit(solution)/shard_map/all_gather | solution.py:83
  11.8 128.7 %all-gather.11.cloned.1.call-start = ((), (), s32[]{:S(2)}) async-start(), calls=%async_computation.4 | async-start | bytes 1327104 | tf_op jit(solution)/shard_map/all_gather | solution.py:72
  12.5 158.6 %reduce-scatter.3.cloned.1.call-start = ((), (), s32[]{:S(2)}) async-start(), calls=%async_computation.5 | async-start | bytes 1966080 | tf_op jit(solution)/shard_map/reduce_scatter | solution.py:92
  144.0 27.1 %copy-start = (bf16[1,128,1536]{2,1,0:T(8,128)(2,1)S(1)}, bf16[1,128,1536]{2,1,0:T(8,128)(2,1)}, u32[]{:S(2)}) copy-start(bf16[1,128,1536]{2,1,0:T(8,128)(2,1)} %param.9) | copy-start | bytes 1179652
  144.0 28.6 %copy-start.2 = (f32[1536]{0:T(1024)S(1)}, f32[1536]{0:T(1024)}, u32[]{:S(2)}) copy-start(f32[1536]{0:T(1024)} %param.12) | copy-start | bytes 18436
  144.0 30.5 %copy-start.1 = (bf16[31,384]{1,0:T(8,128)(2,1)S(1)}, bf16[31,384]{1,0:T(8,128)(2,1)}, u32[]{:S(2)}) copy-start(bf16[31,384]{1,0:T(8,128)(2,1)} %param.16) | copy-start | bytes 71428
  144.0 81.5 %all-gather.15.cloned.1.call-start = ((), (), s32[]{:S(2)}) async-start(), calls=%async_computation.7 | async-start | bytes 2654208 | tf_op jit(solution)/shard_map/all_gather | solution.py:73
  144.6 100.6 %all-gather.13.cloned.1.call-start = ((), (), s32[]{:S(2)}) async-start(), calls=%async_computation.6 | async-start | bytes 1966080 | tf_op jit(solution)/shard_map/all_gather | solution.py:103
  173.6 115.1 %all-gather.17.cloned.1.call-start = ((), (), s32[]{:S(2)}) async-start(), calls=%async_computation.8 | async-start | bytes 1327104 | tf_op jit(solution)/shard_map/all_gather | solution.py:74
  174.4 151.3 %reduce-scatter.5.cloned.1.call-start = ((), (), s32[]{:S(2)}) async-start(), calls=%async_computation.9 | async-start | bytes 1966080 | tf_op jit(solution)/shard_map/reduce_scatter | solution.py:114
Sparse Core Ops, SparseCore 0:
  9.5 67.8 all-gather.8
  79.0 18.1 all-gather.6
  99.4 41.0 all-gather.10
  144.1 26.9 reduce-scatter.2
  173.3 52.0 all-gather.14
  227.0 18.1 all-gather.12
  247.6 41.0 all-gather.16
  298.7 26.9 reduce-scatter.4
where the time goes:
time: 335 us; the launch traced here: 334 us
  waiting for transfers between devices  271 us (81%)
  matrix products  27.2 us (8%)
  between operations  13.6 us (4%)
  local copies, waits for them, and re-layouts  12.4 us (4%)
  other arithmetic  9.88 us (3%)
    all_gather x1, waiting for transfers between devices, on_device(): qkv_local = lax.all_gather(w_qkv, 'dp', axis=0, tiled=True)  64.4 us
    all_gather x1, waiting for transfers between devices, on_device(): glu_local = lax.all_gather(w_glu, 'dp', axis=0, tiled=True)  50.6 us
    all_gather x1, waiting for transfers between devices, on_device(): proj_local = lax.all_gather(w_proj, 'dp', axis=1, tiled=True)  40.5 us
    all_gather x1, waiting for transfers between devices, on_device(): out_local = lax.all_gather(w_out, 'dp', axis=1, tiled=True)  31.5 us
    reduce_scatter x1, waiting for transfers between devices, on_device(): lax.psum_scatter(jnp.dot(rows_here, proj_local, preferred_element_type=jn...  27.1 us
    reduce_scatter x1, waiting for transfers between devices, on_device(): lax.psum_scatter(jnp.dot(rows_here, out_local, preferred_element_type=jnp...  26.5 us
    all_gather x1, waiting for transfers between devices, on_device(): shard_piece = lax.all_gather(normed2, 'seq', axis=0, tiled=True)  14.1 us
    all_gather x1, waiting for transfers between devices, on_device(): lax.all_gather(normed1, 'seq', axis=0, tiled=True)  13.6 us
  transfers between devices with their start and end apart: 8, of which 8 were waited for; matrix products, arithmetic and copies ran while one was open for 10% of the time, Pallas kernels for 0%

commit v1 on v0

--- a/solution.py
+++ b/solution.py
@@ -70,7 +70,12 @@
     kernel_reach = dw_kernel.shape[0] // 2
     qkv_local = lax.all_gather(w_qkv, "dp", axis=0, tiled=True)
     out_local = lax.all_gather(w_out, "dp", axis=1, tiled=True)
-    glu_local = lax.all_gather(w_glu, "dp", axis=0, tiled=True)
+    ring = [w_glu]
+    for hop in range(7):
+        ring.append(lax.ppermute(ring[-1], "dp", [(dev, (dev + 1) % 8) for dev in range(8)]))
+    glu_local = jnp.roll(
+        jnp.concatenate(ring[::-1], axis=0), (lax.axis_index("dp") + 1) * ring[0].shape[0], axis=0
+    )
     proj_local = lax.all_gather(w_proj, "dp", axis=1, tiled=True)
     qkv_matrix = qkv_local.reshape(model_width, 3 * group_width)
     glu_matrix = glu_local.reshape(model_width, 2 * group_width)

time: 335 us -> 328 us (0.979)
  waiting for transfers between devices: 271 us -> 254 us
  other arithmetic: 9.88 us -> 13.3 us
    ppermute x0 -> x7, waiting for transfers between devices: none -> 90.3 us  [on_device(): lax.ppermute(ring[-1], 'dp', [(dev, (dev + 1) % 8) for dev in range(8)])]
    all_gather x1 -> x0, waiting for transfers between devices: 50.6 us -> none  [on_device(): glu_local = lax.all_gather(w_glu, 'dp', axis=0, tiled=True)]
    all_gather x1, waiting for transfers between devices: 40.5 us -> 0.02 us  [on_device(): proj_local = lax.all_gather(w_proj, 'dp', axis=1, tiled=True)]
    all_gather x1, waiting for transfers between devices: 14.1 us -> 0.01 us  [on_device(): shard_piece = lax.all_gather(normed2, 'seq', axis=0, tiled=True)]
    concatenate x0 -> x1, local copies, waits for them, and re-layouts: none -> 8.07 us  [on_device(): jnp.roll(jnp.concatenate(ring[::-1], axis=0), (lax.axis_index('dp') + 1)...]
    reshape x1 -> x0, local copies, waits for them, and re-layouts: 5.64 us -> none  [on_device(): glu_matrix = glu_local.reshape(model_width, 2 * group_width)]
  transfers between devices with their start and end apart: 8 -> 14, of which waited for: 8 -> 12; matrix products, arithmetic and copies ran while one was open for 10% -> 12% of each run, Pallas kernels for 0% -> 0%
where the time goes in v1:
time: 328 us; the launch traced here: 327 us
  waiting for transfers between devices  254 us (77%)
  matrix products  28.8 us (9%)
  local copies, waits for them, and re-layouts  15.5 us (5%)
  between operations  14 us (4%)
  other arithmetic  13.3 us (4%)
    ppermute x7, waiting for transfers between devices, on_device(): lax.ppermute(ring[-1], 'dp', [(dev, (dev + 1) % 8) for dev in range(8)])  90.3 us
    all_gather x1, waiting for transfers between devices, on_device(): qkv_local = lax.all_gather(w_qkv, 'dp', axis=0, tiled=True)  64.4 us
    all_gather x1, waiting for transfers between devices, on_device(): out_local = lax.all_gather(w_out, 'dp', axis=1, tiled=True)  31.6 us
    reduce_scatter x1, waiting for transfers between devices, on_device(): lax.psum_scatter(jnp.dot(rows_here, out_local, preferred_element_type=jnp...  27 us
    reduce_scatter x1, waiting for transfers between devices, on_device(): lax.psum_scatter(jnp.dot(rows_here, proj_local, preferred_element_type=jn...  25.3 us
    all_gather x1, waiting for transfers between devices, on_device(): lax.all_gather(normed1, 'seq', axis=0, tiled=True)  13.6 us
    dot_general x1, matrix products, on_device(): jnp.dot(rows_here, proj_local, preferred_element_type=jnp.float32)  10.5 us
    concatenate x1, local copies, waits for them, and re-layouts, on_device(): jnp.roll(jnp.concatenate(ring[::-1], axis=0), (lax.axis_index('dp') + 1)...  8.07 us
  transfers between devices with their start and end apart: 14, of which 12 were waited for; matrix products, arithmetic and copies ran while one was open for 12% of the time, Pallas kernels for 0%

profile of v1, /device:TPU:0, one launch (start us, length us, event | category | flops | bytes accessed | tf_op | source)
XLA Modules:
  0.0 327.1 jit_solution(2715544496995799083)
XLA Ops:
  6.5 0.7 all-gather.8.cloned.1.call-update
  7.3 0.0 all-gather.6.cloned.1.call-start
  7.3 1.1 convert_reduce_fusion.1
  8.4 1.2 fusion.20
  9.7 2.0 fusion.22
  11.8 0.0 all-gather.10.cloned.1.call-start
  11.8 0.7 all-gather.10.cloned.1.call-update
  12.5 0.0 reduce-scatter.3.cloned.1.call-start
  12.6 0.2 reduce-window.8
  12.7 0.1 convert_reduce_fusion.3
  12.8 0.2 broadcast_compare_fusion
  13.0 64.4 %all-gather.8.cloned.1.call-done = bf16[1536,3,384]{2,0,1:T(8,128)(2,1)} async-done(((bf16[192,3,384]{2,0,1:T(8,128)(2,1)}), bf16[1536,3,384]{2,0,1:T(8,128)(2,1)}) %all-gather.8.cloned.1.call-update) | async-done | bytes 3538960 | tf_op jit(solution)/shard_map/all_gather | solution.py:71
  77.5 6.1 %copy.26 = bf16[1536,3,384]{0,2,1:T(8,128)(2,1)} copy(bf16[1536,3,384]{2,0,1:T(8,128)(2,1)} %all-gather.8.cloned.1.call-done) | data formatting | bytes 7077888 | tf_op jit(solution)/shard_map/all_gather | solution.py:71
  83.6 13.6 %all-gather.6.cloned.1.call-done = bf16[512,1536]{1,0:T(8,128)(2,1)} async-done(((bf16[128,1536]{1,0:T(8,128)(2,1)}), bf16[512,1536]{1,0:T(8,128)(2,1)}) %all-gather.6.cloned.1.call-update) | async-done | bytes 1572880 | tf_op jit(solution)/shard_map/all_gather | solution.py:88
  97.2 4.7 %convolution_convert_fusion = bf16[512,1152]{1,0:T(8,128)(2,1)S(1)} fusion(bf16[512,1536]{1,0:T(8,128)(2,1)} %all-gather.6.cloned.1.call-done, bf16[1536,1152]{0,1:T(8,128)(2,1)} %bitcast.70), kind=kOutput, calls=%fused_computation.5 | convolution fusion | flops 1812529152 | bytes 6291456 | tf_op jit(solution)/shard_map/dot_general | solution.py:87
  101.9 0.6 copy.27
  102.5 3.6 %fusion.42 = (f32[4,512]{1,0:T(4,128)S(1)}, f32[4,512,512]{1,2,0:T(8,128)}) fusion(pred[512,512]{0,1:T(8,128)(4,1)S(1)} %broadcast_compare_fusion, bf16[512,3,4,96]{0,3,2,1:T(8,128)(2,1)S(1)} %bitcast.71), kind=kOutput, calls=%fused_computation.132 | convolution fusion | flops 205521408 | bytes 5251072 | tf_op jit(solution)/shard_map/while/body/eval_jaxpr/sub | solution.py:40
  106.2 2.8 fusion.10
  108.9 31.6 %all-gather.10.cloned.1.call-done = bf16[384,1536]{0,1:T(8,128)(2,1)} async-done(((bf16[384,192]{0,1:T(8,128)(2,1)}), bf16[384,1536]{0,1:T(8,128)(2,1)}) %all-gather.10.cloned.1.call-update) | async-done | bytes 1179664 | tf_op jit(solution)/shard_map/all_gather | solution.py:72
  140.5 3.5 %convolution_convert_fusion.2 = bf16[512,1536]{1,0:T(8,128)(2,1)} fusion(bf16[512,384]{0,1:T(8,128)(2,1)S(1)} %bitcast.73, bf16[384,1536]{0,1:T(8,128)(2,1)} %all-gather.10.cloned.1.call-done), kind=kOutput, calls=%fused_computation.7 | convolution fusion | flops 604766208 | bytes 3145728 | tf_op jit(solution)/shard_map/dot_general | solution.py:98
  144.0 0.0 all-gather.12.cloned.1.call-start
  144.0 27.0 %reduce-scatter.3.cloned.1.call-done = bf16[128,1536]{1,0:T(8,128)(2,1)} async-done(((bf16[512,1536]{1,0:T(8,128)(2,1)}), bf16[128,1536]{1,0:T(8,128)(2,1)}) %reduce-scatter.3.cloned.1.call-update) | async-done | bytes 393232 | tf_op jit(solution)/shard_map/reduce_scatter | solution.py:97
  171.1 1.2 convert_reduce_fusion
  172.3 0.3 fusion.17
  172.6 1.0 fusion.19
  173.6 0.0 all-gather.14.cloned.1.call-start
  173.7 0.3 copy.29
  173.9 1.5 collective-permute-start
  175.5 12.1 %collective-permute-done = bf16[192,2,384]{0,2,1:T(8,128)(2,1)S(1)} collective-permute-done((bf16[192,2,384]{0,2,1:T(8,128)(2,1)S(1)}, bf16[192,2,384]{0,2,1:T(8,128)(2,1)S(1)}, u32[]{:S(2)}, u32[]{:S(2)}) %collective-permute-start) | collective-permute-done | bytes 294944 | tf_op jit(solution)/shard_map/ppermute | solution.py:75
  187.5 12.6 %collective-permute-done.1 = bf16[192,2,384]{0,2,1:T(8,128)(2,1)S(1)} collective-permute-done((bf16[192,2,384]{0,2,1:T(8,128)(2,1)S(1)}, bf16[192,2,384]{0,2,1:T(8,128)(2,1)S(1)}, u32[]{:S(2)}, u32[]{:S(2)}) %collective-permute-start.1) | collective-permute-done | bytes 294944 | tf_op jit(solution)/shard_map/ppermute | solution.py:75
  200.2 0.0 reduce-scatter.5.cloned.1.call-start
  200.2 11.7 %collective-permute-done.2 = bf16[192,2,384]{0,2,1:T(8,128)(2,1)S(1)} collective-permute-done((bf16[192,2,384]{0,2,1:T(8,128)(2,1)S(1)}, bf16[192,2,384]{0,2,1:T(8,128)(2,1)S(1)}, u32[]{:S(2)}, u32[]{:S(2)}) %collective-permute-start.2) | collective-permute-done | bytes 294944 | tf_op jit(solution)/shard_map/ppermute | solution.py:75
  211.9 15.5 %collective-permute-done.3 = bf16[192,2,384]{0,2,1:T(8,128)(2,1)S(1)} collective-permute-done((bf16[192,2,384]{0,2,1:T(8,128)(2,1)S(1)}, bf16[192,2,384]{0,2,1:T(8,128)(2,1)S(1)}, u32[]{:S(2)}, u32[]{:S(2)}) %collective-permute-start.3) | collective-permute-done | bytes 294944 | tf_op jit(solution)/shard_map/ppermute | solution.py:75
  227.5 0.7 convert_reduce_fusion.34
  228.2 20.3 %collective-permute-done.4 = bf16[192,2,384]{0,2,1:T(8,128)(2,1)S(1)} collective-permute-done((bf16[192,2,384]{0,2,1:T(8,128)(2,1)S(1)}, bf16[192,2,384]{0,2,1:T(8,128)(2,1)S(1)}, u32[]{:S(2)}, u32[]{:S(2)}) %collective-permute-start.4) | collective-permute-done | bytes 294944 | tf_op jit(solution)/shard_map/ppermute | solution.py:75
  248.5 0.1 convert_reduce_fusion.2
  248.6 0.7 slice_compare_fusion.29
  249.3 10.0 %collective-permute-done.5 = bf16[192,2,384]{0,2,1:T(8,128)(2,1)S(1)} collective-permute-done((bf16[192,2,384]{0,2,1:T(8,128)(2,1)S(1)}, bf16[192,2,384]{0,2,1:T(8,128)(2,1)S(1)}, u32[]{:S(2)}, u32[]{:S(2)}) %collective-permute-start.5) | collective-permute-done | bytes 294944 | tf_op jit(solution)/shard_map/ppermute | solution.py:75
  259.3 1.6 convert_reduce_fusion.33
  260.9 0.7 slice_compare_fusion.30
  261.6 8.1 %collective-permute-done.6 = bf16[192,2,384]{0,2,1:T(8,128)(2,1)S(1)} collective-permute-done((bf16[192,2,384]{0,2,1:T(8,128)(2,1)S(1)}, bf16[192,2,384]{0,2,1:T(8,128)(2,1)S(1)}, u32[]{:S(2)}, u32[]{:S(2)}) %collective-permute-start.6) | collective-permute-done | bytes 294944 | tf_op jit(solution)/shard_map/ppermute | solution.py:75
  269.7 8.1 %concatenate.6 = bf16[3072,2,384]{0,2,1:T(8,128)(2,1)} concatenate(bf16[192,2,384]{0,2,1:T(8,128)(2,1)S(1)} %collective-permute-done.6, bf16[192,2,384]{0,2,1:T(8,128)(2,1)S(1)} %collective-permute-done.5, bf16[192,2,384]{0,2,1:T(8,128)(2,1)S(1)} %collective-permute-done.4, bf16[192,2,384]{0,2,1:T(8,128)(2,1)S(1)} %collective-permute-done.3, ...), dimensions={0} | concatenate | bytes 9437184 | tf_op jit(solution)/shard_map/jit(_roll_dynamic)/concatenate | solution.py:76
  277.8 3.7 %fusion.2 = f32[512,2,384]{2,0,1:T(8,128)S(1)} fusion(bf16[3072,2,384]{0,2,1:T(8,128)(2,1)} %concatenate.6, s32[]{:T(128)S(6)} %select_n.114, bf16[512,1536]{1,0:T(8,128)(2,1)} %all-gather.12.cloned.1.call-done), kind=kOutput, calls=%fused_computation.8 | convolution fusion | flops 1207959552 | bytes 5505028 | tf_op jit(solution)/shard_map/dot_general | solution.py:109
  281.9 0.2 fusion.33
  282.2 0.0 copy-done.6
  282.6 10.5 %convolution_convert_fusion.1 = bf16[512,1536]{1,0:T(8,128)(2,1)} fusion(bf16[384,1536]{0,1:T(8,128)(2,1)} %all-gather.14.cloned.1.call-done, bf16[512,384]{1,0:T(8,128)(2,1)S(1)} %fusion.33, f32[384]{0:T(512)S(1)} %copy-done.30, f32[384]{0:T(512)S(1)} %copy-done.31, f32[384]{0:T(512)S(1)} %get-tuple-element.18, f32[384]{0:T(512)S(1)} %get-tuple-element.19, ...), kind=kOutput, calls=%fused_computation.6 | convolution fusion | flops 629932032 | bytes 3209216 | tf_op jit(solution)/shard_map/dot_general | solution.py:120
  293.1 25.3 %reduce-scatter.5.cloned.1.call-done = bf16[128,1536]{1,0:T(8,128)(2,1)} async-done(((bf16[512,1536]{1,0:T(8,128)(2,1)}), bf16[128,1536]{1,0:T(8,128)(2,1)}) %reduce-scatter.5.cloned.1.call-update) | async-done | bytes 393232 | tf_op jit(solution)/shard_map/reduce_scatter | solution.py:119
  318.4 1.8 fusion.32
  (108 shorter events, 0.5 us)
Async XLA Ops:
  6.5 6.0 %copy-start.44 = (s32[1,4]{1,0:T(1,128)S(1)}, s32[1,4]{1,0:T(1,128)}, u32[]{:S(2)}) copy-start(s32[1,4]{1,0:T(1,128)} %param.10) | copy-start | bytes 52
  6.5 70.9 %all-gather.8.cloned.1.call-start = ((), (), s32[]{:S(2)}) async-start(), calls=%async_computation.3 | async-start | bytes 3981312 | tf_op jit(solution)/shard_map/all_gather | solution.py:71
  7.3 89.9 %all-gather.6.cloned.1.call-start = ((), (), s32[]{:S(2)}) async-start(), calls=%async_computation.2 | async-start | bytes 1966080 | tf_op jit(solution)/shard_map/all_gather | solution.py:88
  11.8 128.7 %all-gather.10.cloned.1.call-start = ((), (), s32[]{:S(2)}) async-start(), calls=%async_computation.4 | async-start | bytes 1327104 | tf_op jit(solution)/shard_map/all_gather | solution.py:72
  12.5 158.6 %reduce-scatter.3.cloned.1.call-start = ((), (), s32[]{:S(2)}) async-start(), calls=%async_computation.5 | async-start | bytes 1966080 | tf_op jit(solution)/shard_map/reduce_scatter | solution.py:97
  143.9 27.1 %copy-start = (bf16[1,128,1536]{2,1,0:T(8,128)(2,1)S(1)}, bf16[1,128,1536]{2,1,0:T(8,128)(2,1)}, u32[]{:S(2)}) copy-start(bf16[1,128,1536]{2,1,0:T(8,128)(2,1)} %param.9) | copy-start | bytes 1179652
  143.9 28.6 %copy-start.3 = (f32[1536]{0:T(1024)S(1)}, f32[1536]{0:T(1024)}, u32[]{:S(2)}) copy-start(f32[1536]{0:T(1024)} %param.12) | copy-start | bytes 18436
  144.0 29.7 %copy-start.1 = (bf16[192,2,384]{2,1,0:T(2,128)(2,1)S(1)}, bf16[192,2,384]{2,1,0:T(2,128)(2,1)}, u32[]{:S(2)}) copy-start(bf16[192,2,384]{2,1,0:T(2,128)(2,1)} %param.15) | copy-start | bytes 884740
  144.0 83.5 %copy-start.2 = (bf16[31,384]{1,0:T(8,128)(2,1)S(1)}, bf16[31,384]{1,0:T(8,128)(2,1)}, u32[]{:S(2)}) copy-start(bf16[31,384]{1,0:T(8,128)(2,1)} %param.16) | copy-start | bytes 71428
  144.0 133.8 %all-gather.12.cloned.1.call-start = ((), (), s32[]{:S(2)}) async-start(), calls=%async_computation.6 | async-start | bytes 1966080 | tf_op jit(solution)/shard_map/all_gather | solution.py:108
  173.6 108.5 %all-gather.14.cloned.1.call-start = ((), (), s32[]{:S(2)}) async-start(), calls=%async_computation.7 | async-start | bytes 1327104 | tf_op jit(solution)/shard_map/all_gather | solution.py:79
  173.9 13.6 %collective-permute-start = (bf16[192,2,384]{0,2,1:T(8,128)(2,1)S(1)}, bf16[192,2,384]{0,2,1:T(8,128)(2,1)S(1)}, u32[]{:S(2)}, u32[]{:S(2)}) collective-permute-start(bf16[192,2,384]{0,2,1:T(8,128)(2,1)S(1)} %copy.29), channel_id=1, source_target_pairs={{0,4},{4,8},{8,12},{12,16},{16,20},{20,24},{24,28},{28,0},{1,5},{5... | collective-permute-start | bytes 884744 | tf_op jit(solution)/shard_map/ppermute | solution.py:75
  187.5 12.7 %collective-permute-start.1 = (bf16[192,2,384]{0,2,1:T(8,128)(2,1)S(1)}, bf16[192,2,384]{0,2,1:T(8,128)(2,1)S(1)}, u32[]{:S(2)}, u32[]{:S(2)}) collective-permute-start(bf16[192,2,384]{0,2,1:T(8,128)(2,1)S(1)} %collective-permute-done), channel_id=1, source_target_pairs={{0,4},{4,8},{8,12},{12,16},{16,20},{20,24},{24,28},{28,0},{1,5},{5... | collective-permute-start | bytes 884744 | tf_op jit(solution)/shard_map/ppermute | solution.py:75
  200.2 11.8 %collective-permute-start.2 = (bf16[192,2,384]{0,2,1:T(8,128)(2,1)S(1)}, bf16[192,2,384]{0,2,1:T(8,128)(2,1)S(1)}, u32[]{:S(2)}, u32[]{:S(2)}) collective-permute-start(bf16[192,2,384]{0,2,1:T(8,128)(2,1)S(1)} %collective-permute-done.1), channel_id=1, source_target_pairs={{0,4},{4,8},{8,12},{12,16},{16,20},{20,24},{24,28},{28,0},{1,5},{5... | collective-permute-start | bytes 884744 | tf_op jit(solution)/shard_map/ppermute | solution.py:75
  200.2 118.2 %reduce-scatter.5.cloned.1.call-start = ((), (), s32[]{:S(2)}) async-start(), calls=%async_computation.8 | async-start | bytes 1966080 | tf_op jit(solution)/shard_map/reduce_scatter | solution.py:119
  211.9 15.5 %collective-permute-start.3 = (bf16[192,2,384]{0,2,1:T(8,128)(2,1)S(1)}, bf16[192,2,384]{0,2,1:T(8,128)(2,1)S(1)}, u32[]{:S(2)}, u32[]{:S(2)}) collective-permute-start(bf16[192,2,384]{0,2,1:T(8,128)(2,1)S(1)} %collective-permute-done.2), channel_id=1, source_target_pairs={{0,4},{4,8},{8,12},{12,16},{16,20},{20,24},{24,28},{28,0},{1,5},{5... | collective-permute-start | bytes 884744 | tf_op jit(solution)/shard_map/ppermute | solution.py:75
  227.5 21.0 %collective-permute-start.4 = (bf16[192,2,384]{0,2,1:T(8,128)(2,1)S(1)}, bf16[192,2,384]{0,2,1:T(8,128)(2,1)S(1)}, u32[]{:S(2)}, u32[]{:S(2)}) collective-permute-start(bf16[192,2,384]{0,2,1:T(8,128)(2,1)S(1)} %collective-permute-done.3), channel_id=1, source_target_pairs={{0,4},{4,8},{8,12},{12,16},{16,20},{20,24},{24,28},{28,0},{1,5},{5... | collective-permute-start | bytes 884744 | tf_op jit(solution)/shard_map/ppermute | solution.py:75
  248.5 10.8 %collective-permute-start.5 = (bf16[192,2,384]{0,2,1:T(8,128)(2,1)S(1)}, bf16[192,2,384]{0,2,1:T(8,128)(2,1)S(1)}, u32[]{:S(2)}, u32[]{:S(2)}) collective-permute-start(bf16[192,2,384]{0,2,1:T(8,128)(2,1)S(1)} %collective-permute-done.4), channel_id=1, source_target_pairs={{0,4},{4,8},{8,12},{12,16},{16,20},{20,24},{24,28},{28,0},{1,5},{5... | collective-permute-start | bytes 884744 | tf_op jit(solution)/shard_map/ppermute | solution.py:75
  259.3 10.5 %collective-permute-start.6 = (bf16[192,2,384]{0,2,1:T(8,128)(2,1)S(1)}, bf16[192,2,384]{0,2,1:T(8,128)(2,1)S(1)}, u32[]{:S(2)}, u32[]{:S(2)}) collective-permute-start(bf16[192,2,384]{0,2,1:T(8,128)(2,1)S(1)} %collective-permute-done.5), channel_id=1, source_target_pairs={{0,4},{4,8},{8,12},{12,16},{16,20},{20,24},{24,28},{28,0},{1,5},{5... | collective-permute-start | bytes 884744 | tf_op jit(solution)/shard_map/ppermute | solution.py:75
  281.5 0.7 copy-start.4
  281.5 0.7 copy-start.5
  281.5 0.7 copy-start.6
  281.5 0.7 copy-start.7
  281.5 0.7 copy-start.8
  281.6 0.7 copy-start.9
  281.6 0.7 copy-start.10
  281.6 0.7 copy-start.11
  281.6 0.7 copy-start.12
  281.6 0.7 copy-start.18
  281.7 0.7 copy-start.19
  281.7 0.7 copy-start.20
  281.7 0.7 copy-start.21
  281.7 0.7 copy-start.22
  281.7 0.7 copy-start.24
  281.7 0.7 copy-start.25
  281.7 0.7 copy-start.26
  281.7 0.7 copy-start.27
  281.7 0.7 copy-start.28
  281.8 0.7 copy-start.30
  281.8 0.7 copy-start.31
  281.8 0.7 copy-start.33
  281.8 0.7 copy-start.34
  281.8 0.7 copy-start.35
  281.8 0.7 copy-start.36
  281.8 0.7 copy-start.37
  281.8 0.7 copy-start.38
  281.9 0.7 copy-start.40
  281.9 0.7 copy-start.41
  (11 other events, 7.4 us)
Sparse Core Ops, SparseCore 0:
  9.5 67.8 all-gather.7
  79.0 18.1 all-gather.5
  99.4 41.0 all-gather.9
  144.1 26.9 reduce-scatter.2
  173.7 19.6 all-gather.11
  200.3 47.9 all-gather.13
  293.2 25.1 reduce-scatter.4
